TPU v7x, 512 devices: a whole 4x4x16 slice. The times are simulated.
512 devices in a mesh: seg: 32 (over z, core), row: 16 (over x, y).
Axes of the slice: x: 4, y: 4, z: 16, core: 2. Of those that a mesh axis runs over, the one named last changes fastest.
Arguments:
- basis: bfloat16 [32, 8192, 1024], P('seg', 'row'), may hold values from -6 to 6
- arriving: bfloat16 [8192, 1024], P('row'), may hold values from -6 to 6
- blocks: bfloat16 [32, 8192, 256], P('seg', 'row'), may hold values from -8 to 8
- pattern: int32 [32, 128, 4], P('seg', 'row'), may hold values from 0 to 127, as said below
- growth: float32 [32, 1024], P('seg'), may hold values from -6 to 6
Outputs:
- next_basis: bfloat16 [32, 8192, 1024], P('seg', 'row')
- next_growth: float32 [32, 1024], P('seg')
Inputs may be any that keep to these rules, and one draw needn't show every extreme that they name: `pattern`: entry 0 of block row r is r itself; entry 1 is the block 4 positions before or after r on the cycle of 128 blocks; the other entries are distinct blocks fewer than 4 positions from r and not r.
All inputs are finite; a program needn't handle non-finite values.
Results may differ from a plain program's by a relative error of at most 0.0053.
Values may be sent and summed in bfloat16 or wider, within the bound.
No kernel may reach another device: no remote copies, remote signals or barrier semaphores. Data moves between devices by JAX's collectives and lax.ppermute only.
A program may use at most 128 MiB of HBM per device.

v0:
```python
import jax
import jax.numpy as jnp
from jax import lax
from jax.sharding import PartitionSpec as P

BS = 64
NB = 4
REACH = 4


def padded_2(block, sides, width):
    for axis, dim in sides:
        count = lax.axis_size(axis)
        forward = [(i, i + 1) for i in range(count - 1)]
        forward.append((count - 1, 0))
        backward = [(target, source) for source, target in forward]
        low = lax.ppermute(
            lax.slice_in_dim(block, block.shape[dim] - width, None, axis=dim), axis, forward
        )
        high = lax.ppermute(lax.slice_in_dim(block, 0, width, axis=dim), axis, backward)
        block = jnp.concatenate([low, block, high], axis=dim)
    return block


def shifted(array, axis, by):
    length = lax.axis_size(axis)
    pairs = [(i, i + by) for i in range(length) if 0 <= i + by < length]
    return lax.ppermute(array, axis, pairs)


def body(basis, arriving, blocks, pattern, growth):
    row_count = basis.shape[1]
    col_count = basis.shape[2]
    row_blocks = row_count // BS
    total_blocks = row_blocks * lax.axis_size("row")
    padded = padded_2(basis[0], (("row", 0),), REACH * BS)
    tile_stack = padded.reshape(row_blocks + 2 * REACH, BS, col_count)
    local_ids = jnp.arange(row_blocks, dtype=jnp.int32)
    own_blocks = lax.axis_index("row") * row_blocks + local_ids
    offsets = (pattern[0] - own_blocks[:, None] + REACH) % total_blocks
    picked = jnp.take(tile_stack, local_ids[:, None] + offsets, axis=0)
    values = blocks[0].reshape(row_blocks, BS, NB, BS)
    propagated = jnp.einsum("rinj,rnjk->rik", values, picked, preferred_element_type=jnp.float32)
    propagated = propagated.reshape(row_count, col_count).astype(jnp.bfloat16)
    partial_value = lax.dot_general(
        propagated, propagated, (((0,), (0,)), ((), ())), preferred_element_type=jnp.float32
    )
    gram_matrix = lax.psum(partial_value, "row")
    gram_matrix = gram_matrix / (row_count * lax.axis_size("row"))
    factor = jnp.linalg.cholesky(gram_matrix)
    next_growth = growth + jnp.log(jnp.diagonal(factor))[None, :]
    wide_rows = propagated.astype(jnp.float32)
    first_section = lax.axis_index("seg") == 0
    renewed = lax.linalg.triangular_solve(
        factor, wide_rows, left_side=False, lower=True, transpose_a=True
    )
    received = shifted(renewed.astype(jnp.bfloat16)[None], "seg", 1)
    next_basis = jnp.where(first_section, arriving[None], received)
    return (next_basis, next_growth)


def solution(mesh):
    return jax.shard_map(
        body,
        mesh=mesh,
        in_specs=(
            P("seg", "row", None),
            P("row", None),
            P("seg", "row", None),
            P("seg", "row", None),
            P("seg", None),
        ),
        out_specs=(P("seg", "row", None), P("seg", None)),
        check_vma=False,
    )
```

profile of v0, /device:TPU:1, one launch (start us, length us, event | category | flops | bytes accessed | tf_op | source)
XLA Modules:
  0.0 577.8 jit_solution(9313028965769077689)
XLA Ops:
  8.5 4.0 collective-permute-start
  12.5 5.6 collective-permute-start.1
  28.3 3.5 bitcast_convert_fusion
  31.8 3.3 convolution_bitcast_fusion
  35.5 143.7 %all-reduce.3.cloned.1.call-done = f32[1024,1024]{0,1:T(8,128)} async-done(((f32[1024,1024]{0,1:T(8,128)}), f32[1024,1024]{0,1:T(8,128)}) %all-reduce.3.cloned.1.call-update) | async-done | bytes 4194320 | tf_op jit(solution)/shard_map/psum | solution.py:48
  179.2 5.0 broadcast_multiply_fusion
  184.2 5.8 %copy.19 = f32[1024,1024]{1,0:T(8,128)} copy(f32[1024,1024]{0,1:T(8,128)} %broadcast_multiply_fusion) | data formatting | bytes 8388608 | tf_op jit(solution)/shard_map/div | solution.py:49
  190.0 4.4 fusion
  196.4 11.7 %cholesky.223 = f32[128,128]{1,0:T(8,128)S(1)} custom-call(f32[128,128]{1,0:T(8,128)S(1)} %cholesky.580), custom_call_target="Cholesky" | custom-call | tf_op jit(solution)/shard_map/jit(cholesky)/cholesky | solution.py:50
  208.2 9.8 %custom-call.62 = f32[1,128,128]{1,2,0:T(8,128)S(1)} custom-call(f32[1,128,128]{2,1,0:T(8,128)S(1)} %get-tuple-element.66), custom_call_target="InvertDiagBlocksLowerTriangular" | custom-call | tf_op jit(solution)/shard_map/jit(cholesky)/cholesky | solution.py:50
  224.4 11.9 %cholesky.244 = f32[128,128]{1,0:T(8,128)S(1)} custom-call(f32[128,128]{1,0:T(8,128)S(1)} %cholesky.584), custom_call_target="Cholesky" | custom-call | tf_op jit(solution)/shard_map/jit(cholesky)/cholesky | solution.py:50
  236.9 9.8 %custom-call.63 = f32[1,128,128]{1,2,0:T(8,128)S(1)} custom-call(f32[1,128,128]{2,1,0:T(8,128)S(1)} %get-tuple-element.63), custom_call_target="InvertDiagBlocksLowerTriangular" | custom-call | tf_op jit(solution)/shard_map/jit(cholesky)/cholesky | solution.py:50
  250.1 11.7 %cholesky.468 = f32[128,128]{1,0:T(8,128)S(1)} custom-call(f32[128,128]{1,0:T(8,128)S(1)} %cholesky.589), custom_call_target="Cholesky" | custom-call | tf_op jit(solution)/shard_map/jit(cholesky)/cholesky | solution.py:50
  263.1 9.8 %custom-call.64 = f32[1,128,128]{1,2,0:T(8,128)S(1)} custom-call(f32[1,128,128]{2,1,0:T(8,128)S(1)} %get-tuple-element.60), custom_call_target="InvertDiagBlocksLowerTriangular" | custom-call | tf_op jit(solution)/shard_map/jit(cholesky)/cholesky | solution.py:50
  276.4 11.9 %cholesky.487 = f32[128,128]{1,0:T(8,128)S(1)} custom-call(f32[128,128]{1,0:T(8,128)S(1)} %cholesky.594), custom_call_target="Cholesky" | custom-call | tf_op jit(solution)/shard_map/jit(cholesky)/cholesky | solution.py:50
  289.6 9.8 %custom-call.65 = f32[1,128,128]{1,2,0:T(8,128)S(1)} custom-call(f32[1,128,128]{2,1,0:T(8,128)S(1)} %get-tuple-element.57), custom_call_target="InvertDiagBlocksLowerTriangular" | custom-call | tf_op jit(solution)/shard_map/jit(cholesky)/cholesky | solution.py:50
  302.9 11.7 %cholesky.506 = f32[128,128]{1,0:T(8,128)S(1)} custom-call(f32[128,128]{1,0:T(8,128)S(1)} %cholesky.599), custom_call_target="Cholesky" | custom-call | tf_op jit(solution)/shard_map/jit(cholesky)/cholesky | solution.py:50
  316.0 10.2 %custom-call.66 = f32[1,128,128]{1,2,0:T(8,128)S(1)} custom-call(f32[1,128,128]{2,1,0:T(8,128)S(1)} %get-tuple-element.54), custom_call_target="InvertDiagBlocksLowerTriangular" | custom-call | tf_op jit(solution)/shard_map/jit(cholesky)/cholesky | solution.py:50
  329.5 11.7 %cholesky.526 = f32[128,128]{1,0:T(8,128)S(1)} custom-call(f32[128,128]{1,0:T(8,128)S(1)} %cholesky.604), custom_call_target="Cholesky" | custom-call | tf_op jit(solution)/shard_map/jit(cholesky)/cholesky | solution.py:50
  342.5 9.8 %custom-call.67 = f32[1,128,128]{1,2,0:T(8,128)S(1)} custom-call(f32[1,128,128]{2,1,0:T(8,128)S(1)} %get-tuple-element.51), custom_call_target="InvertDiagBlocksLowerTriangular" | custom-call | tf_op jit(solution)/shard_map/jit(cholesky)/cholesky | solution.py:50
  355.3 11.9 %cholesky.546 = f32[128,128]{1,0:T(8,128)S(1)} custom-call(f32[128,128]{1,0:T(8,128)S(1)} %cholesky.609), custom_call_target="Cholesky" | custom-call | tf_op jit(solution)/shard_map/jit(cholesky)/cholesky | solution.py:50
  368.4 9.8 %custom-call.68 = f32[1,128,128]{1,2,0:T(8,128)S(1)} custom-call(f32[1,128,128]{2,1,0:T(8,128)S(1)} %get-tuple-element.48), custom_call_target="InvertDiagBlocksLowerTriangular" | custom-call | tf_op jit(solution)/shard_map/jit(cholesky)/cholesky | solution.py:50
  380.9 11.7 %cholesky.564 = f32[128,128]{1,0:T(8,128)S(1)} custom-call(f32[128,128]{1,0:T(8,128)S(1)} %convolution_subtract_fusion.13), custom_call_target="Cholesky" | custom-call | tf_op jit(solution)/shard_map/jit(cholesky)/cholesky | solution.py:50
  399.5 6.6 %fusion.1 = (f32[1024,1024]{1,0:T(8,128)}, f32[1024,1024]{1,0:T(8,128)}) fusion(f32[1024,1024]{1,0:T(8,128)} %get-tuple-element.46, pred[]{:T(512)S(6)} %cholesky.579), kind=kLoop, calls=%fused_computation.8 | loop fusion | flops 4194304 | bytes 12582913 | tf_op jit(solution)/shard_map/triangular_solve | solution.py:54
  406.2 27.3 %while.1 = (s32[]{:T(128)}, f32[1024,1024]{1,0:T(8,128)}, s32[8,2]{0,1:T(2,128)S(1)}, f32[8,128,128]{2,1,0:T(8,128)}, s32[]{:T(128)}) while((s32[]{:T(128)}, f32[1024,1024]{1,0:T(8,128)}, s32[8,2]{0,1:T(2,128)S(1)}, f32[8,128,128]{2,1,0:T(8,128)}, s32[]{:T(128)}) %tuple.61), condition=%wide.while_cond, body=%wide.while_body.sunk | while | flops 2 | bytes 132205 | solution.py:54
  427.3 2.8 bitcast_dynamic-update-slice_fusion.9
  433.4 79.6 %custom-call.69 = f32[8,128,128]{1,2,0:T(8,128)S(1)} custom-call(f32[8,128,128]{2,1,0:T(8,128)} %get-tuple-element.9), custom_call_target="InvertDiagBlocksLowerTriangular" | custom-call | tf_op jit(solution)/shard_map/triangular_solve | solution.py:54
  528.3 3.2 convolution_subtract_fusion.4
  533.6 3.6 convolution_subtract_fusion.7
  539.2 4.3 convolution_subtract_fusion.3
  545.5 4.1 collective-permute-start.2
  550.1 17.3 %gather_fusion.1 = f32[1024]{0:T(1024)S(1)} fusion(f32[1024,1024]{1,0:T(8,128)} %get-tuple-element.23, s32[1024]{0:T(1024)S(1)} %bitcast.159), kind=kCustom, calls=%fused_computation.1 | custom fusion | bytes 16384 | tf_op jit(solution)/shard_map/jit(diagonal)/cond/branch_0_fun/gather | solution.py:51
  (115 shorter events, 98.0 us)
Async XLA Ops:
  7.2 172.0 %all-reduce.3.cloned.1.call-start = ((), (), s32[]{:S(2)}) async-start(), calls=%async_computation | async-start | bytes 8388608 | tf_op jit(solution)/shard_map/psum | solution.py:48
  8.5 14.2 %collective-permute-start = (bf16[256,1024]{1,0:T(8,128)(2,1)S(1)}, bf16[256,1024]{1,0:T(8,128)(2,1)S(1)}, u32[]{:S(2)}, u32[]{:S(2)}) collective-permute-start(bf16[256,1024]{1,0:T(8,128)(2,1)S(1)} %get-tuple-element.26), channel_id=1, source_target_pairs={{0,1},{1,2},{2,3},{3,4},{4,5},{5,6},{6,7},{7,8},{8,9},{9,10},{10,1... | collective-permute-start | bytes 1572872 | tf_op jit(solution)/shard_map/ppermute | solution.py:17
  12.5 11.7 %collective-permute-start.1 = (bf16[256,1024]{1,0:T(8,128)(2,1)S(1)}, bf16[256,1024]{1,0:T(8,128)(2,1)S(1)}, u32[]{:S(2)}, u32[]{:S(2)}) collective-permute-start(bf16[256,1024]{1,0:T(8,128)(2,1)S(1)} %get-tuple-element.27), channel_id=1, source_target_pairs={{1,0},{2,1},{3,2},{4,3},{5,4},{6,5},{7,6},{8,7},{9,8},{10,9},{11,1... | collective-permute-start | bytes 1572872 | tf_op jit(solution)/shard_map/ppermute | solution.py:20
  31.8 3.3 copy-start.1
  194.5 1.9 copy-start
  513.0 13.8 %copy-start.3 = (f32[8,128,128]{1,2,0:T(8,128)}, f32[8,128,128]{1,2,0:T(8,128)S(1)}, u32[]{:S(2)}) copy-start(f32[8,128,128]{1,2,0:T(8,128)S(1)} %custom-call.69) | copy-start | bytes 1572868
  531.6 18.0 %copy-start.2 = (bf16[512,1024]{1,0:T(8,128)(2,1)S(1)}, bf16[512,1024]{1,0:T(8,128)(2,1)}, u32[]{:S(2)}) copy-start(bf16[512,1024]{1,0:T(8,128)(2,1)} %param.6) | copy-start | bytes 3145732
  543.5 23.9 %copy-start.4 = (f32[1,1024]{1,0:T(1,128)S(1)}, f32[1,1024]{1,0:T(1,128)}, u32[]{:S(2)}) copy-start(f32[1,1024]{1,0:T(1,128)} %param.9) | copy-start | bytes 12292
  545.5 22.6 %collective-permute-start.2 = (bf16[1,512,1024]{1,2,0:T(8,128)(2,1)}, bf16[1,512,1024]{1,2,0:T(8,128)(2,1)}, u32[]{:S(2)}, u32[]{:S(2)}) collective-permute-start(bf16[1,512,1024]{1,2,0:T(8,128)(2,1)} %fusion.9), channel_id=1, source_target_pairs={{0,16},{16,32},{32,48},{48,64},{64,80},{80,96},{96,112},{112,128},... | collective-permute-start | bytes 3145736 | tf_op jit(solution)/shard_map/ppermute | solution.py:28
Sparse Core Ops, SparseCore 0:
  35.2 143.8 all-reduce.2
where the time goes:
time: 584 us; the launch traced here: 578 us
  other arithmetic  273 us (47%)
  waiting for transfers between devices  146 us (25%)
  local copies, waits for them, and re-layouts  63.6 us (11%)
  matrix products  61.6 us (11%)
  between operations  19.7 us (3%)
  starting transfers between devices  13.7 us (2%)
    another operation x30, other arithmetic, body(): factor = jnp.linalg.cholesky(gram_matrix)  172 us
    psum x1, waiting for transfers between devices, body(): gram_matrix = lax.psum(partial_value, 'row')  144 us
    another operation x3, other arithmetic, body(): lax.linalg.triangular_solve(factor, wide_rows, left_side=False, lower=Tru...  86.2 us
    another operation x15, matrix products, body(): lax.linalg.triangular_solve(factor, wide_rows, left_side=False, lower=Tru...  31.8 us
    another operation x24, local copies, waits for them, and re-layouts  27.3 us
    another operation x14, matrix products, body(): factor = jnp.linalg.cholesky(gram_matrix)  23.1 us
    gather x1, local copies, waits for them, and re-layouts, body(): next_growth = growth + jnp.log(jnp.diagonal(factor))[None, :]  17.3 us
  transfers between devices with their start and end apart: 4, of which 3 were waited for; matrix products, arithmetic and copies ran while one was open for 4% of the time, Pallas kernels for 0%

commit v1 on v0

--- a/solution.py
+++ b/solution.py
@@ -45,7 +45,11 @@
     partial_value = lax.dot_general(
         propagated, propagated, (((0,), (0,)), ((), ())), preferred_element_type=jnp.float32
     )
-    gram_matrix = lax.psum(partial_value, "row")
+    gram_matrix = partial_value
+    for hop in (1, 2, 4, 8):
+        gram_matrix = gram_matrix + lax.ppermute(
+            gram_matrix, "row", [(dev, dev ^ hop) for dev in range(16)]
+        )
     gram_matrix = gram_matrix / (row_count * lax.axis_size("row"))
     factor = jnp.linalg.cholesky(gram_matrix)
     next_growth = growth + jnp.log(jnp.diagonal(factor))[None, :]

time: 584 us -> 813 us (1.39)
  waiting for transfers between devices: 146 us -> 353 us
  starting transfers between devices: 13.7 us -> 39.7 us
  between operations: 19.7 us -> 6.27 us
    ppermute x0 -> x4, waiting for transfers between devices: none -> 351 us  [body(): lax.ppermute(gram_matrix, 'row', [(dev, dev ^ hop) for dev in range(16)])]
    psum x1 -> x0, waiting for transfers between devices: 144 us -> none  [body(): gram_matrix = lax.psum(partial_value, 'row')]
    ppermute x0 -> x4, starting transfers between devices: none -> 21.5 us  [body(): lax.ppermute(gram_matrix, 'row', [(dev, dev ^ hop) for dev in range(16)])]
  transfers between devices with their start and end apart: 4 -> 7, of which waited for: 3 -> 6; matrix products, arithmetic and copies ran while one was open for 4% -> 3% of each run, Pallas kernels for 0% -> 0%
where the time goes in v1:
time: 813 us; the launch traced here: 803 us
  waiting for transfers between devices  353 us (43%)
  other arithmetic  281 us (35%)
  local copies, waits for them, and re-layouts  63.2 us (8%)
  matrix products  59.6 us (7%)
  starting transfers between devices  39.7 us (5%)
    ppermute x4, waiting for transfers between devices, body(): lax.ppermute(gram_matrix, 'row', [(dev, dev ^ hop) for dev in range(16)])  351 us
    another operation x30, other arithmetic, body(): factor = jnp.linalg.cholesky(gram_matrix)  172 us
    another operation x3, other arithmetic, body(): lax.linalg.triangular_solve(factor, wide_rows, left_side=False, lower=Tru...  86.4 us
    another operation x15, matrix products, body(): lax.linalg.triangular_solve(factor, wide_rows, left_side=False, lower=Tru...  31.7 us
    another operation x24, local copies, waits for them, and re-layouts  27.3 us
    another operation x14, matrix products, body(): factor = jnp.linalg.cholesky(gram_matrix)  23 us
    ppermute x4, starting transfers between devices, body(): lax.ppermute(gram_matrix, 'row', [(dev, dev ^ hop) for dev in range(16)])  21.5 us
    gather x1, local copies, waits for them, and re-layouts, body(): next_growth = growth + jnp.log(jnp.diagonal(factor))[None, :]  17.3 us
  transfers between devices with their start and end apart: 7, of which 6 were waited for; matrix products, arithmetic and copies ran while one was open for 3% of the time, Pallas kernels for 0%

profile of v1, /device:TPU:1, one launch (start us, length us, event | category | flops | bytes accessed | tf_op | source)
XLA Modules:
  0.0 803.0 jit_solution(18006855504516361832)
XLA Ops:
  5.9 5.6 collective-permute-start.1
  26.6 6.0 collective-permute-start.2
  32.5 87.2 %collective-permute-done.2 = f32[1024,1024]{0,1:T(8,128)S(1)} collective-permute-done((f32[1024,1024]{0,1:T(8,128)S(1)}, f32[1024,1024]{0,1:T(8,128)S(1)}, u32[]{:S(2)}, u32[]{:S(2)}) %collective-permute-start.2) | collective-permute-done | bytes 4194336 | tf_op jit(solution)/shard_map/ppermute | solution.py:50
  121.1 8.1 %collective-permute-start.3 = (f32[1024,1024]{0,1:T(8,128)S(1)}, f32[1024,1024]{0,1:T(8,128)S(1)}, u32[]{:S(2)}, u32[]{:S(2)}) collective-permute-start(f32[1024,1024]{0,1:T(8,128)S(1)} %add.199), channel_id=1, source_target_pairs={{0,2},{1,3},{2,0},{3,1},{4,6},{5,7},{6,4},{7,5},{8,10},{9,11},{10,... | collective-permute-start | bytes 12582920 | tf_op jit(solution)/shard_map/ppermute | solution.py:50
  129.3 88.5 %collective-permute-done.3 = f32[1024,1024]{0,1:T(8,128)S(1)} collective-permute-done((f32[1024,1024]{0,1:T(8,128)S(1)}, f32[1024,1024]{0,1:T(8,128)S(1)}, u32[]{:S(2)}, u32[]{:S(2)}) %collective-permute-start.3) | collective-permute-done | bytes 4194336 | tf_op jit(solution)/shard_map/ppermute | solution.py:50
  222.3 87.9 %collective-permute-done.4 = f32[1024,1024]{0,1:T(8,128)S(1)} collective-permute-done((f32[1024,1024]{0,1:T(8,128)S(1)}, f32[1024,1024]{0,1:T(8,128)S(1)}, u32[]{:S(2)}, u32[]{:S(2)}) %collective-permute-start.4) | collective-permute-done | bytes 4194336 | tf_op jit(solution)/shard_map/ppermute | solution.py:50
  313.1 4.3 collective-permute-start.5
  317.8 87.3 %collective-permute-done.5 = f32[1024,1024]{0,1:T(8,128)} collective-permute-done((f32[1024,1024]{0,1:T(8,128)}, f32[1024,1024]{0,1:T(8,128)}, u32[]{:S(2)}, u32[]{:S(2)}) %collective-permute-start.5) | collective-permute-done | bytes 4194336 | tf_op jit(solution)/shard_map/ppermute | solution.py:50
  405.1 6.9 add_multiply_fusion
  412.0 5.5 copy.21
  417.5 4.4 fusion
  423.9 11.7 %cholesky.223 = f32[128,128]{1,0:T(8,128)S(1)} custom-call(f32[128,128]{1,0:T(8,128)S(1)} %cholesky.580), custom_call_target="Cholesky" | custom-call | tf_op jit(solution)/shard_map/jit(cholesky)/cholesky | solution.py:54
  435.6 9.8 %custom-call.62 = f32[1,128,128]{1,2,0:T(8,128)S(1)} custom-call(f32[1,128,128]{2,1,0:T(8,128)S(1)} %get-tuple-element.66), custom_call_target="InvertDiagBlocksLowerTriangular" | custom-call | tf_op jit(solution)/shard_map/jit(cholesky)/cholesky | solution.py:54
  451.9 11.9 %cholesky.244 = f32[128,128]{1,0:T(8,128)S(1)} custom-call(f32[128,128]{1,0:T(8,128)S(1)} %cholesky.584), custom_call_target="Cholesky" | custom-call | tf_op jit(solution)/shard_map/jit(cholesky)/cholesky | solution.py:54
  464.4 9.8 %custom-call.63 = f32[1,128,128]{1,2,0:T(8,128)S(1)} custom-call(f32[1,128,128]{2,1,0:T(8,128)S(1)} %get-tuple-element.63), custom_call_target="InvertDiagBlocksLowerTriangular" | custom-call | tf_op jit(solution)/shard_map/jit(cholesky)/cholesky | solution.py:54
  477.6 11.7 %cholesky.468 = f32[128,128]{1,0:T(8,128)S(1)} custom-call(f32[128,128]{1,0:T(8,128)S(1)} %cholesky.589), custom_call_target="Cholesky" | custom-call | tf_op jit(solution)/shard_map/jit(cholesky)/cholesky | solution.py:54
  490.6 9.8 %custom-call.64 = f32[1,128,128]{1,2,0:T(8,128)S(1)} custom-call(f32[1,128,128]{2,1,0:T(8,128)S(1)} %get-tuple-element.60), custom_call_target="InvertDiagBlocksLowerTriangular" | custom-call | tf_op jit(solution)/shard_map/jit(cholesky)/cholesky | solution.py:54
  503.9 12.1 %cholesky.487 = f32[128,128]{1,0:T(8,128)S(1)} custom-call(f32[128,128]{1,0:T(8,128)S(1)} %cholesky.594), custom_call_target="Cholesky" | custom-call | tf_op jit(solution)/shard_map/jit(cholesky)/cholesky | solution.py:54
  517.3 9.8 %custom-call.65 = f32[1,128,128]{1,2,0:T(8,128)S(1)} custom-call(f32[1,128,128]{2,1,0:T(8,128)S(1)} %get-tuple-element.57), custom_call_target="InvertDiagBlocksLowerTriangular" | custom-call | tf_op jit(solution)/shard_map/jit(cholesky)/cholesky | solution.py:54
  530.6 11.7 %cholesky.506 = f32[128,128]{1,0:T(8,128)S(1)} custom-call(f32[128,128]{1,0:T(8,128)S(1)} %cholesky.599), custom_call_target="Cholesky" | custom-call | tf_op jit(solution)/shard_map/jit(cholesky)/cholesky | solution.py:54
  543.7 9.9 %custom-call.66 = f32[1,128,128]{1,2,0:T(8,128)S(1)} custom-call(f32[1,128,128]{2,1,0:T(8,128)S(1)} %get-tuple-element.54), custom_call_target="InvertDiagBlocksLowerTriangular" | custom-call | tf_op jit(solution)/shard_map/jit(cholesky)/cholesky | solution.py:54
  556.9 11.7 %cholesky.526 = f32[128,128]{1,0:T(8,128)S(1)} custom-call(f32[128,128]{1,0:T(8,128)S(1)} %cholesky.604), custom_call_target="Cholesky" | custom-call | tf_op jit(solution)/shard_map/jit(cholesky)/cholesky | solution.py:54
  569.9 9.8 %custom-call.67 = f32[1,128,128]{1,2,0:T(8,128)S(1)} custom-call(f32[1,128,128]{2,1,0:T(8,128)S(1)} %get-tuple-element.51), custom_call_target="InvertDiagBlocksLowerTriangular" | custom-call | tf_op jit(solution)/shard_map/jit(cholesky)/cholesky | solution.py:54
  582.7 11.9 %cholesky.546 = f32[128,128]{1,0:T(8,128)S(1)} custom-call(f32[128,128]{1,0:T(8,128)S(1)} %cholesky.609), custom_call_target="Cholesky" | custom-call | tf_op jit(solution)/shard_map/jit(cholesky)/cholesky | solution.py:54
  595.9 9.8 %custom-call.68 = f32[1,128,128]{1,2,0:T(8,128)S(1)} custom-call(f32[1,128,128]{2,1,0:T(8,128)S(1)} %get-tuple-element.48), custom_call_target="InvertDiagBlocksLowerTriangular" | custom-call | tf_op jit(solution)/shard_map/jit(cholesky)/cholesky | solution.py:54
  608.3 11.7 %cholesky.564 = f32[128,128]{1,0:T(8,128)S(1)} custom-call(f32[128,128]{1,0:T(8,128)S(1)} %slice_subtract_fusion.6), custom_call_target="Cholesky" | custom-call | tf_op jit(solution)/shard_map/jit(cholesky)/cholesky | solution.py:54
  627.0 6.6 fusion.1
  633.6 27.3 %while.1 = (s32[]{:T(128)}, f32[1024,1024]{1,0:T(8,128)}, s32[8,2]{0,1:T(2,128)S(1)}, f32[8,128,128]{2,1,0:T(8,128)}, s32[]{:T(128)}) while((s32[]{:T(128)}, f32[1024,1024]{1,0:T(8,128)}, s32[8,2]{0,1:T(2,128)S(1)}, f32[8,128,128]{2,1,0:T(8,128)}, s32[]{:T(128)}) %tuple.61), condition=%wide.while_cond, body=%wide.while_body.sunk | while | flops 2 | bytes 132205 | solution.py:58
  660.9 79.8 %custom-call.69 = f32[8,128,128]{1,2,0:T(8,128)S(1)} custom-call(f32[8,128,128]{2,1,0:T(8,128)} %get-tuple-element.9), custom_call_target="InvertDiagBlocksLowerTriangular" | custom-call | tf_op jit(solution)/shard_map/triangular_solve | solution.py:58
  766.8 4.3 convolution_subtract_fusion
  773.0 8.6 %collective-permute-start.6 = (bf16[1,512,1024]{1,2,0:T(8,128)(2,1)}, bf16[1,512,1024]{1,2,0:T(8,128)(2,1)}, u32[]{:S(2)}, u32[]{:S(2)}) collective-permute-start(bf16[1,512,1024]{1,2,0:T(8,128)(2,1)} %fusion.9), channel_id=1, source_target_pairs={{0,16},{16,32},{32,48},{48,64},{64,80},{80,96},{96,112},{112,128},... | collective-permute-start | bytes 3145736 | tf_op jit(solution)/shard_map/ppermute | solution.py:28
  782.2 17.3 %gather_fusion.1 = f32[1024]{0:T(1024)S(1)} fusion(f32[1024,1024]{1,0:T(8,128)} %get-tuple-element.23, s32[1024]{0:T(1024)S(1)} %bitcast.161), kind=kCustom, calls=%fused_computation.1 | custom fusion | bytes 16384 | tf_op jit(solution)/shard_map/jit(diagonal)/cond/branch_0_fun/gather | solution.py:55
  (123 shorter events, 125.1 us)
Async XLA Ops:
  1.9 14.2 %collective-permute-start = (bf16[256,1024]{1,0:T(8,128)(2,1)S(1)}, bf16[256,1024]{1,0:T(8,128)(2,1)S(1)}, u32[]{:S(2)}, u32[]{:S(2)}) collective-permute-start(bf16[256,1024]{1,0:T(8,128)(2,1)S(1)} %get-tuple-element.26), channel_id=1, source_target_pairs={{0,1},{1,2},{2,3},{3,4},{4,5},{5,6},{6,7},{7,8},{8,9},{9,10},{10,1... | collective-permute-start | bytes 1572872 | tf_op jit(solution)/shard_map/ppermute | solution.py:17
  5.9 11.7 %collective-permute-start.1 = (bf16[256,1024]{1,0:T(8,128)(2,1)S(1)}, bf16[256,1024]{1,0:T(8,128)(2,1)S(1)}, u32[]{:S(2)}, u32[]{:S(2)}) collective-permute-start(bf16[256,1024]{1,0:T(8,128)(2,1)S(1)} %get-tuple-element.27), channel_id=1, source_target_pairs={{1,0},{2,1},{3,2},{4,3},{5,4},{6,5},{7,6},{8,7},{9,8},{10,9},{11,1... | collective-permute-start | bytes 1572872 | tf_op jit(solution)/shard_map/ppermute | solution.py:20
  25.2 292.3 %copy-start.1 = (bf16[8,1024,64]{1,2,0:T(8,128)(2,1)}, bf16[8,1024,64]{1,2,0:T(8,128)(2,1)S(1)}, u32[]{:S(2)}) copy-start(bf16[8,1024,64]{1,2,0:T(8,128)(2,1)S(1)} %bitcast_convert_fusion) | copy-start | bytes 3145732
  26.6 93.2 %collective-permute-start.2 = (f32[1024,1024]{0,1:T(8,128)S(1)}, f32[1024,1024]{0,1:T(8,128)S(1)}, u32[]{:S(2)}, u32[]{:S(2)}) collective-permute-start(f32[1024,1024]{0,1:T(8,128)S(1)} %convolution_bitcast_fusion), channel_id=1, source_target_pairs={{0,1},{1,0},{2,3},{3,2},{4,5},{5,4},{6,7},{7,6},{8,9},{9,8},{10,11... | collective-permute-start | bytes 12582920 | tf_op jit(solution)/shard_map/ppermute | solution.py:50
  121.1 96.7 %collective-permute-start.3 = (f32[1024,1024]{0,1:T(8,128)S(1)}, f32[1024,1024]{0,1:T(8,128)S(1)}, u32[]{:S(2)}, u32[]{:S(2)}) collective-permute-start(f32[1024,1024]{0,1:T(8,128)S(1)} %add.199), channel_id=1, source_target_pairs={{0,2},{1,3},{2,0},{3,1},{4,6},{5,7},{6,4},{7,5},{8,10},{9,11},{10,... | collective-permute-start | bytes 12582920 | tf_op jit(solution)/shard_map/ppermute | solution.py:50
  219.2 91.1 %collective-permute-start.4 = (f32[1024,1024]{0,1:T(8,128)S(1)}, f32[1024,1024]{0,1:T(8,128)S(1)}, u32[]{:S(2)}, u32[]{:S(2)}) collective-permute-start(f32[1024,1024]{0,1:T(8,128)S(1)} %add.200), channel_id=1, source_target_pairs={{0,4},{1,5},{2,6},{3,7},{4,0},{5,1},{6,2},{7,3},{8,12},{9,13},{10,... | collective-permute-start | bytes 12582920 | tf_op jit(solution)/shard_map/ppermute | solution.py:50
  313.1 92.0 %collective-permute-start.5 = (f32[1024,1024]{0,1:T(8,128)}, f32[1024,1024]{0,1:T(8,128)}, u32[]{:S(2)}, u32[]{:S(2)}) collective-permute-start(f32[1024,1024]{0,1:T(8,128)} %add.201), channel_id=1, source_target_pairs={{0,8},{1,9},{2,10},{3,11},{4,12},{5,13},{6,14},{7,15},{8,0},{9,1},... | collective-permute-start | bytes 12582920 | tf_op jit(solution)/shard_map/ppermute | solution.py:50
  421.9 1.9 copy-start
  740.7 13.8 %copy-start.3 = (f32[8,128,128]{1,2,0:T(8,128)}, f32[8,128,128]{1,2,0:T(8,128)S(1)}, u32[]{:S(2)}) copy-start(f32[8,128,128]{1,2,0:T(8,128)S(1)} %custom-call.69) | copy-start | bytes 1572868
  759.2 22.4 %copy-start.2 = (bf16[512,1024]{1,0:T(8,128)(2,1)S(1)}, bf16[512,1024]{1,0:T(8,128)(2,1)}, u32[]{:S(2)}) copy-start(bf16[512,1024]{1,0:T(8,128)(2,1)} %param.6) | copy-start | bytes 3145732
  771.1 28.4 %copy-start.4 = (f32[1,1024]{1,0:T(1,128)S(1)}, f32[1,1024]{1,0:T(1,128)}, u32[]{:S(2)}) copy-start(f32[1,1024]{1,0:T(1,128)} %param.9) | copy-start | bytes 12292
  773.0 27.1 %collective-permute-start.6 = (bf16[1,512,1024]{1,2,0:T(8,128)(2,1)}, bf16[1,512,1024]{1,2,0:T(8,128)(2,1)}, u32[]{:S(2)}, u32[]{:S(2)}) collective-permute-start(bf16[1,512,1024]{1,2,0:T(8,128)(2,1)} %fusion.9), channel_id=1, source_target_pairs={{0,16},{16,32},{32,48},{48,64},{64,80},{80,96},{96,112},{112,128},... | collective-permute-start | bytes 3145736 | tf_op jit(solution)/shard_map/ppermute | solution.py:28
